TPU v7x, 32 devices: a whole 2x2x4 slice. The times are simulated.
32 devices in a mesh: gx: 8 (over z, y), gy: 4 (over x, core).
Axes of the slice: x: 2, y: 2, z: 4, core: 2. Of those that a mesh axis runs over, the one named last changes fastest.
Arguments:
- conc_prev: float32 [128, 64, 128], P('gx', 'gy'), may hold values from 0.5 to 2
- right_side: float32 [128, 64, 128], P('gx', 'gy'), may hold values from -5 to 7
- soil_id: int32 [128, 64, 128], P('gx', 'gy'), may hold values from 0 to 7
- soil_table: float32 [5, 8], replicated, may hold values from 0.3 to 3
Outputs:
- correction: float32 [128, 64, 128], P('gx', 'gy')
All inputs are finite; a program needn't handle non-finite values.
Results may differ from a plain program's by a relative error of at most 0.00002.
Values sent between devices are 32-bit elements; how exact they have to be, the bound alone decides.
No kernel may reach another device: no remote copies, remote signals or barrier semaphores. Data moves between devices by JAX's collectives and lax.ppermute only.
A program may use at most 128 MiB of HBM per device.

v0:
```python
import jax
import jax.numpy as jnp
from jax import lax
from jax.sharding import PartitionSpec as P

CHEB = 3
COARSE_SWEEPS = 8
storage_scale = 0.05
cheb_centre = 1.1
cheb_half = 0.9
cheb_ratio = cheb_centre / cheb_half
jacobi_weight = 0.8


def padded_2(cells, sides, width):
    for axis, dim in sides:
        count = lax.axis_size(axis)
        ends = count - 1
        head = lax.slice_in_dim(cells, 0, width, axis=dim)
        tail = lax.slice_in_dim(cells, cells.shape[dim] - width, cells.shape[dim], axis=dim)
        cells = jnp.concatenate(
            [
                lax.ppermute(tail, axis, [(i, (i + 1) % count) for i in range(ends)]),
                cells,
                lax.ppermute(head, axis, [((i + 1) % count, i) for i in range(ends)]),
            ],
            axis=dim,
        )
    return cells


def harmonic(first, second):
    return first * second / jnp.maximum(0.5 * (first + second), 0.1)


def face_terms(coeffs, spacing):
    eastward = coeffs[0]
    northward = coeffs[1]
    upward = coeffs[2]
    centre_x = eastward[1:-1, 1:-1]
    centre_y = northward[1:-1, 1:-1]
    centre_z = upward[1:-1, 1:-1]
    east_face = harmonic(eastward[2:, 1:-1], centre_x) * spacing
    west_face = harmonic(eastward[:-2, 1:-1], centre_x) * spacing
    north_face = harmonic(northward[1:-1, 2:], centre_y) * spacing
    south_face = harmonic(northward[1:-1, :-2], centre_y) * spacing
    vertical = harmonic(centre_z[:, :, 1:], centre_z[:, :, :-1]) * spacing
    closed = jnp.zeros_like(centre_z[:, :, :1])
    above_face = jnp.concatenate([vertical, closed], axis=2)
    below_face = jnp.concatenate([closed, vertical], axis=2)
    storage = coeffs[3, 1:-1, 1:-1]
    return (east_face, west_face, north_face, south_face, above_face, below_face, storage)


def main_diagonal(coeffs, spacing):
    east_face, west_face, north_face, south_face, above_face, below_face, storage = face_terms(
        coeffs, spacing
    )
    return jnp.maximum(
        storage + east_face + west_face + north_face + south_face + above_face + below_face, 0.01
    )


def operate(values, coeffs, spacing):
    east_face, west_face, north_face, south_face, above_face, below_face, storage = face_terms(
        coeffs, spacing
    )
    centre = values[1:-1, 1:-1]
    upper_cell = jnp.concatenate([centre[:, :, 1:], centre[:, :, :1]], axis=2)
    lower_cell = jnp.concatenate([centre[:, :, -1:], centre[:, :, :-1]], axis=2)
    fluxes = east_face * (centre - values[2:, 1:-1]) + west_face * (centre - values[:-2, 1:-1])
    fluxes = (
        fluxes
        + north_face * (centre - values[1:-1, 2:])
        + south_face * (centre - values[1:-1, :-2])
    )
    fluxes = fluxes + above_face * (centre - upper_cell) + below_face * (centre - lower_cell)
    return storage * centre + fluxes


def coarsen(values):
    lead = values.shape[:-3]
    size_x, size_y, size_z = values.shape[-3:]
    split = values.reshape(lead + (size_x // 2, 2, size_y // 2, 2, size_z // 2, 2))
    return jnp.mean(split, axis=(-5, -3, -1))


def prolong(values):
    return jnp.repeat(jnp.repeat(jnp.repeat(values, 2, axis=0), 2, axis=1), 2, axis=2)


def shrink(values, amount):
    if amount == 0:
        return values
    return values[..., amount:-amount, amount:-amount, :]


def tile_halo(layers, amount):
    return padded_2(layers, (("gx", 1), ("gy", 2)), amount)


def expand(values):
    return (tile_halo(values[None], 1)[0], 1)


def smooth(target, target_margin, initial, coeffs, coeff_margin, spacing):
    if initial is None:
        current = target_margin
        diagonal = main_diagonal(shrink(coeffs, coeff_margin - current - 1), spacing)
        update = target / diagonal * (1.0 / cheb_centre)
        iterate = update
    else:
        padded, padded_margin = expand(initial)
        applied = operate(padded, shrink(coeffs, coeff_margin - padded_margin), spacing)
        current = padded_margin - 1
        diagonal = main_diagonal(shrink(coeffs, coeff_margin - current - 1), spacing)
        misfit = shrink(target, target_margin - current) - applied
        update = misfit / diagonal * (1.0 / cheb_centre)
        iterate = shrink(padded, 1) + update
    diagonal_margin = current
    factor = 1.0 / cheb_ratio
    for repeat in range(CHEB - 1):
        padded, padded_margin = expand(iterate)
        applied = operate(padded, shrink(coeffs, coeff_margin - padded_margin), spacing)
        next_margin = padded_margin - 1
        misfit = shrink(target, target_margin - next_margin) - applied
        factor_new = 1.0 / (2.0 * cheb_ratio - factor)
        update = factor_new * factor * shrink(
            update, current - next_margin
        ) + 2.0 * factor_new / cheb_half * (
            misfit / shrink(diagonal, diagonal_margin - next_margin)
        )
        iterate = shrink(iterate, current - next_margin) + update
        current = next_margin
        factor = factor_new
    return (iterate, current)


def leftover(target, target_margin, iterate, coeffs, coeff_margin, spacing):
    padded, padded_margin = expand(iterate)
    applied = operate(padded, shrink(coeffs, coeff_margin - padded_margin), spacing)
    return shrink(target, target_margin - padded_margin + 1) - applied


def local_fields(conc_prev, soil_id, soil_table):
    fields = []
    for record in range(5):
        looked = jnp.zeros(soil_id.shape, jnp.float32)
        for material in range(soil_table.shape[1]):
            looked = looked + jnp.where(soil_id == material, soil_table[record, material], 0.0)
        fields.append(looked)
    storage = storage_scale * (1.0 + fields[3] * jnp.exp((fields[4] - 1.0) * jnp.log(conc_prev)))
    return jnp.stack([fields[0], fields[1], fields[2], storage])


def local(conc_prev, right_side, soil_id, soil_table):
    halo_depth = 0
    fine_margin = max(4, 2 * halo_depth + 2)
    own_coeffs = local_fields(conc_prev, soil_id, soil_table)
    fine_coeffs = padded_2(own_coeffs, (("gx", 1), ("gy", 2)), fine_margin)
    mid_margin = fine_margin // 2
    mid_coeffs = coarsen(fine_coeffs)
    coarse_coeffs = coarsen(shrink(mid_coeffs, mid_margin - 2))
    fine_iterate, current = smooth(right_side, halo_depth, None, fine_coeffs, fine_margin, 1.0)
    fine_misfit = leftover(right_side, halo_depth, fine_iterate, fine_coeffs, fine_margin, 1.0)
    fine_iterate = shrink(fine_iterate, current)
    mid_plain = coarsen(fine_misfit)
    mid_iterate, current = smooth(mid_plain, halo_depth, None, mid_coeffs, mid_margin, 0.25)
    mid_misfit = leftover(mid_plain, halo_depth, mid_iterate, mid_coeffs, mid_margin, 0.25)
    mid_iterate = shrink(mid_iterate, current)
    coarse_source = coarsen(mid_misfit)
    narrow = coarse_coeffs[:, :, 1:-1]
    group_source, group_coeffs = (
        lax.all_gather(coarse_source, "gy", axis=1, tiled=True),
        lax.all_gather(narrow, "gy", axis=2, tiled=True),
    )
    line_total = jnp.sum(group_source, axis=1)
    line_store = jnp.sum(group_coeffs[3, 1:-1], axis=1)
    line_mean = line_total / line_store
    group_coeffs = jnp.pad(group_coeffs, ((0, 0), (0, 0), (1, 1), (0, 0)))
    diagonal = main_diagonal(group_coeffs, 0.0625)
    coarse_value = jnp.broadcast_to(line_mean[:, None, :], group_source.shape)
    for sweeps in range(COARSE_SWEEPS):
        padded = padded_2(coarse_value, (("gx", 0),), 1)
        padded = jnp.pad(padded, ((0, 0), (1, 1), (0, 0)))
        applied = operate(padded, group_coeffs, 0.0625)
        coarse_value = coarse_value + jacobi_weight * ((group_source - applied) / diagonal)
    tile_width = coarse_source.shape[1]
    coarse_value = lax.dynamic_slice_in_dim(
        coarse_value, lax.axis_index("gy") * tile_width, tile_width, 1
    )
    mid_start = mid_iterate + prolong(coarse_value)
    mid_result, current = smooth(mid_plain, halo_depth, mid_start, mid_coeffs, mid_margin, 0.25)
    fine_start = fine_iterate + prolong(mid_result)
    fine_result, current = smooth(right_side, halo_depth, fine_start, fine_coeffs, fine_margin, 1.0)
    return fine_result


def solution(mesh):
    placed = (P("gx", "gy", None), P("gx", "gy", None), P("gx", "gy", None), P())
    return jax.shard_map(
        local, mesh=mesh, in_specs=placed, out_specs=P("gx", "gy", None), check_vma=False
    )
```

profile of v0, /device:TPU:26, one launch (start us, length us, event | category | flops | bytes accessed | tf_op | source)
XLA Modules:
  0.0 402.7 jit_solution(15851466285160394497)
XLA Ops:
  5.6 6.3 %add_bitcast_fusion.3 = (f32[1,16,16,128]{3,2,1,0:T(8,128)S(1)}, pred[16,16,128]{2,1,0:T(8,128)(4,1)S(1)}, pred[16,16,128]{2,1,0:T(8,128)(4,1)S(1)}, pred[16,16,...) fusion(f32[]{:T(128)} %bitcast.23, f32[]{:T(128)} %bitcast.22, ...), kind=kLoop, calls=%fused_computation.162 | loop fusion | flops 753664 | bytes 524320 | tf_op jit(solution)/shard_map/stack | solution.py:153
  11.9 5.3 %add_bitcast_fusion.1 = f32[1,16,16,128]{3,2,1,0:T(8,128)S(1)} fusion(pred[16,16,128]{2,1,0:T(8,128)(4,1)S(1)} %get-tuple-element.49, pred[16,16,128]{2,1,0:T(8,128)(4,1)S(1)} %get-tuple-element.48, pred[16,16,128]{2,1,0:T(8,128)(4,1)S(1)} %get-tuple-element.47, pred[16,16,128]{2,1,0:T(8,128)(4,1)S(1)} %get-tuple-element.46, ...), kind=kLoop, calls=%fused_computation.160 | loop fusion | flops 491520 | bytes 393248 | tf_op jit(solution)/shard_map/stack | solution.py:153
  17.2 5.0 %add_bitcast_fusion.2 = f32[1,16,16,128]{3,2,1,0:T(8,128)S(1)} fusion(pred[16,16,128]{2,1,0:T(8,128)(4,1)S(1)} %get-tuple-element.49, pred[16,16,128]{2,1,0:T(8,128)(4,1)S(1)} %get-tuple-element.48, pred[16,16,128]{2,1,0:T(8,128)(4,1)S(1)} %get-tuple-element.47, pred[16,16,128]{2,1,0:T(8,128)(4,1)S(1)} %get-tuple-element.46, ...), kind=kLoop, calls=%fused_computation.161 | loop fusion | flops 491520 | bytes 393248 | tf_op jit(solution)/shard_map/stack | solution.py:153
  22.1 10.1 %add_multiply_fusion = f32[16,16,128]{2,1,0:T(8,128)S(1)} fusion(f32[16,16,128]{2,1,0:T(8,128)S(1)} %copy-done.1, pred[16,16,128]{2,1,0:T(8,128)(4,1)S(1)} %get-tuple-element.49, pred[16,16,128]{2,1,0:T(8,128)(4,1)S(1)} %get-tuple-element.48, pred[16,16,128]{2,1,0:T(8,128)(4,1)S(1)} %get-tuple-element.47, pred[16,16,128]{2,1,0:T(8,128)(4,1)S(1)} %get-tuple-element.46, ...), kind=kLoop, calls=%fused_computation.163 | loop fusion | flops 1146880 | bytes 524352 | tf_op jit(solution)/shard_map/mul | solution.py:152
  32.3 3.3 collective-permute-start.1
  39.5 4.0 collective-permute-done
  48.6 3.8 collective-permute-done.2
  53.8 3.2 collective-permute-start.5
  57.0 2.6 collective-permute-start.4
  59.7 3.8 collective-permute-done.4
  72.8 3.9 collective-permute-start.8
  76.7 18.2 %copy.868 = f32[4,24,24,128]{0,3,2,1:T(8,128)} copy(f32[4,24,24,128]{3,2,1,0:T(8,128)S(1)} %pad_maximum_fusion) | data formatting | bytes 2359296 | tf_op jit(solution)/shard_map/concatenate | solution.py:21
  94.9 27.0 %reduce_sum.55 = f32[4,12,12,64]{0,3,2,1:T(8,128)} reduce(f32[4,12,2,12,2,64,2]{0,6,5,4,3,2,1:T(2,128)} %bitcast.161, f32[]{:T(128)} %constant.27.clone.1), dimensions={2,4,6}, to_apply=%region_1.2 | reduce | flops 258048 | bytes 1327108 | tf_op jit(solution)/shard_map/reduce_sum | solution.py:85
  121.9 3.7 copy.869
  133.1 2.8 collective-permute-start.13
  136.0 3.0 collective-permute-start.12
  139.0 3.4 collective-permute-done.12
  149.8 9.8 %reshape.56 = f32[8,2,8,2,64,2]{5,4,3,2,1,0:T(8,128)} reshape(f32[16,16,128]{2,1,0:T(8,128)S(1)} %fusion.41) | data formatting | bytes 262144 | tf_op jit(solution)/shard_map/reshape | solution.py:84
  159.6 4.0 reduce_sum.54
  165.7 4.0 collective-permute-start.16
  169.7 3.1 copy.880
  172.8 5.3 %reduce_sum.58 = f32[4,6,6,32]{0,3,2,1:T(8,128)S(1)} reduce(f32[4,6,2,6,2,32,2]{0,6,5,4,3,2,1:T(2,128)} %bitcast.162, f32[]{:T(128)} %constant.27.clone.1), dimensions={2,4,6}, to_apply=%region_4.5 | reduce | flops 32256 | bytes 165892 | tf_op jit(solution)/shard_map/reduce_sum | solution.py:85
  185.5 2.9 collective-permute-start.21
  188.4 2.9 collective-permute-start.20
  191.3 10.7 %all_gather.7 = f32[4,6,16,32]{0,3,2,1:T(8,128)S(1)} all-gather(f32[4,6,4,32]{0,3,2,1:T(8,128)S(1)} %slice_multiply_fusion), channel_id=1, replica_groups=mesh['gx'=8,'gy'=4] {'gy'}, dimensions={2}, use_global_device_ids=true | all-gather | bytes 61440 | tf_op jit(solution)/shard_map/all_gather | solution.py:175
  202.0 4.6 %collective-permute-start.23 = (f32[1,10,1,64]{3,2,1,0:T(1,128)S(1)}, f32[1,10,1,64]{3,2,1,0:T(1,128)S(1)}, u32[]{:S(2)}, u32[]{:S(2)}) collective-permute-start(f32[1,10,1,64]{3,2,1,0:T(1,128)S(1)} %get-tuple-element.143), channel_id=1, source_target_pairs={{1,0},{2,1},{3,2},{5,4},{6,5},{7,6},{9,8},{10,9},{11,10},{13,12},{... | collective-permute-start | bytes 7688 | tf_op jit(solution)/shard_map/ppermute | solution.py:25
  211.9 3.8 collective-permute-start.25
  217.9 4.3 %collective-permute-done.24 = f32[1,1,8,64]{3,2,1,0:T(8,128)S(1)} collective-permute-done((f32[1,1,8,64]{3,2,1,0:T(8,128)S(1)}, f32[1,1,8,64]{3,2,1,0:T(8,128)S(1)}, u32[]{:S(2)}, u32[]{:S(2)}) %collective-permute-start.24) | collective-permute-done | bytes 2080 | tf_op jit(solution)/shard_map/ppermute | solution.py:23
  230.6 5.2 %all_gather.6 = f32[4,16,32]{2,0,1:T(4,128)S(1)} all-gather(f32[4,4,32]{2,0,1:T(4,128)S(1)} %copy.879), channel_id=1, replica_groups=mesh['gx'=8,'gy'=4] {'gy'}, dimensions={1}, use_global_device_ids=true | all-gather | bytes 10240 | tf_op jit(solution)/shard_map/all_gather | solution.py:174
  237.9 3.9 collective-permute-start.29
  244.7 2.9 collective-permute-start.30
  247.6 2.9 collective-permute-start.31
  250.6 3.4 collective-permute-done.31
  256.2 3.9 collective-permute-start.33
  262.8 2.8 collective-permute-start.34
  265.7 3.0 collective-permute-start.35
  268.8 3.3 collective-permute-done.35
  274.2 3.9 collective-permute-start.37
  282.8 3.9 collective-permute-start.39
  291.4 3.9 collective-permute-start.41
  300.1 3.9 collective-permute-start.43
  309.0 3.9 collective-permute-start.44
  317.3 2.6 collective-permute-start.46
  324.5 3.9 collective-permute-start.48
  340.1 3.9 collective-permute-start.52
  356.6 3.9 collective-permute-start.56
  372.4 3.9 collective-permute-start.60
  388.2 3.9 collective-permute-start.64
  (279 shorter events, 163.1 us)
Async XLA Ops:
  32.3 7.1 %collective-permute-start.1 = (f32[4,4,16,128]{3,2,1,0:T(8,128)S(1)}, f32[4,4,16,128]{3,2,1,0:T(8,128)S(1)}, u32[]{:S(2)}, u32[]{:S(2)}) collective-permute-start(f32[4,4,16,128]{3,2,1,0:T(8,128)S(1)} %get-tuple-element.56), channel_id=1, source_target_pairs={{4,0},{8,4},{12,8},{16,12},{20,16},{24,20},{28,24},{5,1},{9,5},{13... | collective-permute-start | bytes 393224 | tf_op jit(solution)/shard_map/ppermute | solution.py:25
  35.6 7.8 %collective-permute-start = (f32[4,4,16,128]{3,2,1,0:T(8,128)S(1)}, f32[4,4,16,128]{3,2,1,0:T(8,128)S(1)}, u32[]{:S(2)}, u32[]{:S(2)}) collective-permute-start(f32[4,4,16,128]{3,2,1,0:T(8,128)S(1)} %get-tuple-element.55), channel_id=1, source_target_pairs={{0,4},{4,8},{8,12},{12,16},{16,20},{20,24},{24,28},{1,5},{5,9},{9,... | collective-permute-start | bytes 393224 | tf_op jit(solution)/shard_map/ppermute | solution.py:23
  43.5 5.1 %collective-permute-start.3 = (f32[4,24,4,128]{3,1,2,0:T(8,128)S(1)}, f32[4,24,4,128]{3,1,2,0:T(8,128)S(1)}, u32[]{:S(2)}, u32[]{:S(2)}) collective-permute-start(f32[4,24,4,128]{3,1,2,0:T(8,128)S(1)} %copy.913), channel_id=1, source_target_pairs={{1,0},{2,1},{3,2},{5,4},{6,5},{7,6},{9,8},{10,9},{11,10},{13,12},{... | collective-permute-start | bytes 589832 | tf_op jit(solution)/shard_map/ppermute | solution.py:25
  45.5 7.0 %collective-permute-start.2 = (f32[4,24,4,128]{3,1,2,0:T(8,128)S(1)}, f32[4,24,4,128]{3,1,2,0:T(8,128)S(1)}, u32[]{:S(2)}, u32[]{:S(2)}) collective-permute-start(f32[4,24,4,128]{3,1,2,0:T(8,128)S(1)} %copy.912), channel_id=1, source_target_pairs={{0,1},{1,2},{2,3},{4,5},{5,6},{6,7},{8,9},{9,10},{10,11},{12,13},{... | collective-permute-start | bytes 589832 | tf_op jit(solution)/shard_map/ppermute | solution.py:23
  53.8 5.9 %collective-permute-start.5 = (f32[1,1,16,128]{3,2,1,0:T(8,128)S(1)}, f32[1,1,16,128]{3,2,1,0:T(8,128)S(1)}, u32[]{:S(2)}, u32[]{:S(2)}) collective-permute-start(f32[1,1,16,128]{3,2,1,0:T(8,128)S(1)} %get-tuple-element.109), channel_id=1, source_target_pairs={{4,0},{8,4},{12,8},{16,12},{20,16},{24,20},{28,24},{5,1},{9,5},{13... | collective-permute-start | bytes 24584 | tf_op jit(solution)/shard_map/ppermute | solution.py:25
  57.0 6.4 %collective-permute-start.4 = (f32[1,1,16,128]{3,2,1,0:T(8,128)S(1)}, f32[1,1,16,128]{3,2,1,0:T(8,128)S(1)}, u32[]{:S(2)}, u32[]{:S(2)}) collective-permute-start(f32[1,1,16,128]{3,2,1,0:T(8,128)S(1)} %get-tuple-element.108), channel_id=1, source_target_pairs={{0,4},{4,8},{8,12},{12,16},{16,20},{20,24},{24,28},{1,5},{5,9},{9,... | collective-permute-start | bytes 24584 | tf_op jit(solution)/shard_map/ppermute | solution.py:23
  70.9 54.8 %collective-permute-start.9 = (f32[1,1,16,128]{3,2,1,0:T(8,128)S(1)}, f32[1,1,16,128]{3,2,1,0:T(8,128)S(1)}, u32[]{:S(2)}, u32[]{:S(2)}) collective-permute-start(f32[1,1,16,128]{3,2,1,0:T(8,128)S(1)} %get-tuple-element.107), channel_id=1, source_target_pairs={{4,0},{8,4},{12,8},{16,12},{20,16},{24,20},{28,24},{5,1},{9,5},{13... | collective-permute-start | bytes 24584 | tf_op jit(solution)/shard_map/ppermute | solution.py:25
  72.8 52.9 %collective-permute-start.8 = (f32[1,1,16,128]{3,2,1,0:T(8,128)S(1)}, f32[1,1,16,128]{3,2,1,0:T(8,128)S(1)}, u32[]{:S(2)}, u32[]{:S(2)}) collective-permute-start(f32[1,1,16,128]{3,2,1,0:T(8,128)S(1)} %get-tuple-element.106), channel_id=1, source_target_pairs={{0,4},{4,8},{8,12},{12,16},{16,20},{20,24},{24,28},{1,5},{5,9},{9,... | collective-permute-start | bytes 24584 | tf_op jit(solution)/shard_map/ppermute | solution.py:23
  127.6 5.0 %collective-permute-start.10 = (f32[1,18,1,128]{3,2,1,0:T(1,128)S(1)}, f32[1,18,1,128]{3,2,1,0:T(1,128)S(1)}, u32[]{:S(2)}, u32[]{:S(2)}) collective-permute-start(f32[1,18,1,128]{3,2,1,0:T(1,128)S(1)} %get-tuple-element.94), channel_id=1, source_target_pairs={{0,1},{1,2},{2,3},{4,5},{5,6},{6,7},{8,9},{9,10},{10,11},{12,13},{... | collective-permute-start | bytes 27656 | tf_op jit(solution)/shard_map/ppermute | solution.py:23
  133.1 5.9 %collective-permute-start.13 = (f32[1,1,16,128]{3,2,1,0:T(8,128)S(1)}, f32[1,1,16,128]{3,2,1,0:T(8,128)S(1)}, u32[]{:S(2)}, u32[]{:S(2)}) collective-permute-start(f32[1,1,16,128]{3,2,1,0:T(8,128)S(1)} %get-tuple-element.105), channel_id=1, source_target_pairs={{4,0},{8,4},{12,8},{16,12},{20,16},{24,20},{28,24},{5,1},{9,5},{13... | collective-permute-start | bytes 24584 | tf_op jit(solution)/shard_map/ppermute | solution.py:25
  136.0 6.4 %collective-permute-start.12 = (f32[1,1,16,128]{3,2,1,0:T(8,128)S(1)}, f32[1,1,16,128]{3,2,1,0:T(8,128)S(1)}, u32[]{:S(2)}, u32[]{:S(2)}) collective-permute-start(f32[1,1,16,128]{3,2,1,0:T(8,128)S(1)} %get-tuple-element.104), channel_id=1, source_target_pairs={{0,4},{4,8},{8,12},{12,16},{16,20},{20,24},{24,28},{1,5},{5,9},{9,... | collective-permute-start | bytes 24584 | tf_op jit(solution)/shard_map/ppermute | solution.py:23
  144.3 5.0 %collective-permute-start.14 = (f32[1,18,1,128]{3,2,1,0:T(1,128)S(1)}, f32[1,18,1,128]{3,2,1,0:T(1,128)S(1)}, u32[]{:S(2)}, u32[]{:S(2)}) collective-permute-start(f32[1,18,1,128]{3,2,1,0:T(1,128)S(1)} %get-tuple-element.92), channel_id=1, source_target_pairs={{0,1},{1,2},{2,3},{4,5},{5,6},{6,7},{8,9},{9,10},{10,11},{12,13},{... | collective-permute-start | bytes 27656 | tf_op jit(solution)/shard_map/ppermute | solution.py:23
  163.7 14.5 %collective-permute-start.17 = (f32[1,1,8,64]{3,2,1,0:T(8,128)S(1)}, f32[1,1,8,64]{3,2,1,0:T(8,128)S(1)}, u32[]{:S(2)}, u32[]{:S(2)}) collective-permute-start(f32[1,1,8,64]{3,2,1,0:T(8,128)S(1)} %get-tuple-element.201), channel_id=1, source_target_pairs={{4,0},{8,4},{12,8},{16,12},{20,16},{24,20},{28,24},{5,1},{9,5},{13... | collective-permute-start | bytes 6152 | tf_op jit(solution)/shard_map/ppermute | solution.py:25
  165.7 12.5 %collective-permute-start.16 = (f32[1,1,8,64]{3,2,1,0:T(8,128)S(1)}, f32[1,1,8,64]{3,2,1,0:T(8,128)S(1)}, u32[]{:S(2)}, u32[]{:S(2)}) collective-permute-start(f32[1,1,8,64]{3,2,1,0:T(8,128)S(1)} %get-tuple-element.200), channel_id=1, source_target_pairs={{0,4},{4,8},{8,12},{12,16},{16,20},{20,24},{24,28},{1,5},{5,9},{9,... | collective-permute-start | bytes 6152 | tf_op jit(solution)/shard_map/ppermute | solution.py:23
  185.5 16.6 %collective-permute-start.21 = (f32[1,1,8,64]{3,2,1,0:T(8,128)S(1)}, f32[1,1,8,64]{3,2,1,0:T(8,128)S(1)}, u32[]{:S(2)}, u32[]{:S(2)}) collective-permute-start(f32[1,1,8,64]{3,2,1,0:T(8,128)S(1)} %get-tuple-element.199), channel_id=1, source_target_pairs={{4,0},{8,4},{12,8},{16,12},{20,16},{24,20},{28,24},{5,1},{9,5},{13... | collective-permute-start | bytes 6152 | tf_op jit(solution)/shard_map/ppermute | solution.py:25
  188.4 13.6 %collective-permute-start.20 = (f32[1,1,8,64]{3,2,1,0:T(8,128)S(1)}, f32[1,1,8,64]{3,2,1,0:T(8,128)S(1)}, u32[]{:S(2)}, u32[]{:S(2)}) collective-permute-start(f32[1,1,8,64]{3,2,1,0:T(8,128)S(1)} %get-tuple-element.198), channel_id=1, source_target_pairs={{0,4},{4,8},{8,12},{12,16},{16,20},{20,24},{24,28},{1,5},{5,9},{9,... | collective-permute-start | bytes 6152 | tf_op jit(solution)/shard_map/ppermute | solution.py:23
  202.0 8.8 %collective-permute-start.23 = (f32[1,10,1,64]{3,2,1,0:T(1,128)S(1)}, f32[1,10,1,64]{3,2,1,0:T(1,128)S(1)}, u32[]{:S(2)}, u32[]{:S(2)}) collective-permute-start(f32[1,10,1,64]{3,2,1,0:T(1,128)S(1)} %get-tuple-element.143), channel_id=1, source_target_pairs={{1,0},{2,1},{3,2},{5,4},{6,5},{7,6},{9,8},{10,9},{11,10},{13,12},{... | collective-permute-start | bytes 7688 | tf_op jit(solution)/shard_map/ppermute | solution.py:25
  211.9 6.0 %collective-permute-start.25 = (f32[1,1,8,64]{3,2,1,0:T(8,128)S(1)}, f32[1,1,8,64]{3,2,1,0:T(8,128)S(1)}, u32[]{:S(2)}, u32[]{:S(2)}) collective-permute-start(f32[1,1,8,64]{3,2,1,0:T(8,128)S(1)} %get-tuple-element.197), channel_id=1, source_target_pairs={{4,0},{8,4},{12,8},{16,12},{20,16},{24,20},{28,24},{5,1},{9,5},{13... | collective-permute-start | bytes 6152 | tf_op jit(solution)/shard_map/ppermute | solution.py:25
  215.7 6.4 %collective-permute-start.24 = (f32[1,1,8,64]{3,2,1,0:T(8,128)S(1)}, f32[1,1,8,64]{3,2,1,0:T(8,128)S(1)}, u32[]{:S(2)}, u32[]{:S(2)}) collective-permute-start(f32[1,1,8,64]{3,2,1,0:T(8,128)S(1)} %get-tuple-element.196), channel_id=1, source_target_pairs={{0,4},{4,8},{8,12},{12,16},{16,20},{20,24},{24,28},{1,5},{5,9},{9,... | collective-permute-start | bytes 6152 | tf_op jit(solution)/shard_map/ppermute | solution.py:23
  222.2 5.0 %collective-permute-start.27 = (f32[1,10,1,64]{3,2,1,0:T(1,128)S(1)}, f32[1,10,1,64]{3,2,1,0:T(1,128)S(1)}, u32[]{:S(2)}, u32[]{:S(2)}) collective-permute-start(f32[1,10,1,64]{3,2,1,0:T(1,128)S(1)} %get-tuple-element.141), channel_id=1, source_target_pairs={{1,0},{2,1},{3,2},{5,4},{6,5},{7,6},{9,8},{10,9},{11,10},{13,12},{... | collective-permute-start | bytes 7688 | tf_op jit(solution)/shard_map/ppermute | solution.py:25
  235.9 6.0 %collective-permute-start.28 = (f32[1,16,32]{2,1,0:T(8,128)S(1)}, f32[1,16,32]{2,1,0:T(8,128)S(1)}, u32[]{:S(2)}, u32[]{:S(2)}) collective-permute-start(f32[1,16,32]{2,1,0:T(8,128)S(1)} %broadcast_in_dim.284), channel_id=1, source_target_pairs={{4,0},{8,4},{12,8},{16,12},{20,16},{24,20},{28,24},{5,1},{9,5},{13... | collective-permute-start | bytes 6152 | tf_op jit(solution)/shard_map/ppermute | solution.py:25
  237.9 6.4 %collective-permute-start.29 = (f32[1,16,32]{2,1,0:T(8,128)S(1)}, f32[1,16,32]{2,1,0:T(8,128)S(1)}, u32[]{:S(2)}, u32[]{:S(2)}) collective-permute-start(f32[1,16,32]{2,1,0:T(8,128)S(1)} %broadcast_in_dim.285), channel_id=1, source_target_pairs={{0,4},{4,8},{8,12},{12,16},{16,20},{20,24},{24,28},{1,5},{5,9},{9,... | collective-permute-start | bytes 6152 | tf_op jit(solution)/shard_map/ppermute | solution.py:23
  244.7 5.9 %collective-permute-start.30 = (f32[1,16,32]{2,1,0:T(8,128)S(1)}, f32[1,16,32]{2,1,0:T(8,128)S(1)}, u32[]{:S(2)}, u32[]{:S(2)}) collective-permute-start(f32[1,16,32]{2,1,0:T(8,128)S(1)} %get-tuple-element.191), channel_id=1, source_target_pairs={{4,0},{8,4},{12,8},{16,12},{20,16},{24,20},{28,24},{5,1},{9,5},{13... | collective-permute-start | bytes 6152 | tf_op jit(solution)/shard_map/ppermute | solution.py:25
  247.6 6.4 %collective-permute-start.31 = (f32[1,16,32]{2,1,0:T(8,128)S(1)}, f32[1,16,32]{2,1,0:T(8,128)S(1)}, u32[]{:S(2)}, u32[]{:S(2)}) collective-permute-start(f32[1,16,32]{2,1,0:T(8,128)S(1)} %get-tuple-element.190), channel_id=1, source_target_pairs={{0,4},{4,8},{8,12},{12,16},{16,20},{20,24},{24,28},{1,5},{5,9},{9,... | collective-permute-start | bytes 6152 | tf_op jit(solution)/shard_map/ppermute | solution.py:23
  254.3 5.9 %collective-permute-start.32 = (f32[1,16,32]{2,1,0:T(8,128)S(1)}, f32[1,16,32]{2,1,0:T(8,128)S(1)}, u32[]{:S(2)}, u32[]{:S(2)}) collective-permute-start(f32[1,16,32]{2,1,0:T(8,128)S(1)} %get-tuple-element.185), channel_id=1, source_target_pairs={{4,0},{8,4},{12,8},{16,12},{20,16},{24,20},{28,24},{5,1},{9,5},{13... | collective-permute-start | bytes 6152 | tf_op jit(solution)/shard_map/ppermute | solution.py:25
  256.2 6.4 %collective-permute-start.33 = (f32[1,16,32]{2,1,0:T(8,128)S(1)}, f32[1,16,32]{2,1,0:T(8,128)S(1)}, u32[]{:S(2)}, u32[]{:S(2)}) collective-permute-start(f32[1,16,32]{2,1,0:T(8,128)S(1)} %get-tuple-element.184), channel_id=1, source_target_pairs={{0,4},{4,8},{8,12},{12,16},{16,20},{20,24},{24,28},{1,5},{5,9},{9,... | collective-permute-start | bytes 6152 | tf_op jit(solution)/shard_map/ppermute | solution.py:23
  262.8 5.9 %collective-permute-start.34 = (f32[1,16,32]{2,1,0:T(8,128)S(1)}, f32[1,16,32]{2,1,0:T(8,128)S(1)}, u32[]{:S(2)}, u32[]{:S(2)}) collective-permute-start(f32[1,16,32]{2,1,0:T(8,128)S(1)} %get-tuple-element.179), channel_id=1, source_target_pairs={{4,0},{8,4},{12,8},{16,12},{20,16},{24,20},{28,24},{5,1},{9,5},{13... | collective-permute-start | bytes 6152 | tf_op jit(solution)/shard_map/ppermute | solution.py:25
  265.7 6.4 %collective-permute-start.35 = (f32[1,16,32]{2,1,0:T(8,128)S(1)}, f32[1,16,32]{2,1,0:T(8,128)S(1)}, u32[]{:S(2)}, u32[]{:S(2)}) collective-permute-start(f32[1,16,32]{2,1,0:T(8,128)S(1)} %get-tuple-element.178), channel_id=1, source_target_pairs={{0,4},{4,8},{8,12},{12,16},{16,20},{20,24},{24,28},{1,5},{5,9},{9,... | collective-permute-start | bytes 6152 | tf_op jit(solution)/shard_map/ppermute | solution.py:23
  272.3 5.9 %collective-permute-start.36 = (f32[1,16,32]{2,1,0:T(8,128)S(1)}, f32[1,16,32]{2,1,0:T(8,128)S(1)}, u32[]{:S(2)}, u32[]{:S(2)}) collective-permute-start(f32[1,16,32]{2,1,0:T(8,128)S(1)} %get-tuple-element.173), channel_id=1, source_target_pairs={{4,0},{8,4},{12,8},{16,12},{20,16},{24,20},{28,24},{5,1},{9,5},{13... | collective-permute-start | bytes 6152 | tf_op jit(solution)/shard_map/ppermute | solution.py:25
  274.2 6.4 %collective-permute-start.37 = (f32[1,16,32]{2,1,0:T(8,128)S(1)}, f32[1,16,32]{2,1,0:T(8,128)S(1)}, u32[]{:S(2)}, u32[]{:S(2)}) collective-permute-start(f32[1,16,32]{2,1,0:T(8,128)S(1)} %get-tuple-element.172), channel_id=1, source_target_pairs={{0,4},{4,8},{8,12},{12,16},{16,20},{20,24},{24,28},{1,5},{5,9},{9,... | collective-permute-start | bytes 6152 | tf_op jit(solution)/shard_map/ppermute | solution.py:23
  280.9 5.9 %collective-permute-start.38 = (f32[1,16,32]{2,1,0:T(8,128)S(1)}, f32[1,16,32]{2,1,0:T(8,128)S(1)}, u32[]{:S(2)}, u32[]{:S(2)}) collective-permute-start(f32[1,16,32]{2,1,0:T(8,128)S(1)} %get-tuple-element.167), channel_id=1, source_target_pairs={{4,0},{8,4},{12,8},{16,12},{20,16},{24,20},{28,24},{5,1},{9,5},{13... | collective-permute-start | bytes 6152 | tf_op jit(solution)/shard_map/ppermute | solution.py:25
  282.8 6.4 %collective-permute-start.39 = (f32[1,16,32]{2,1,0:T(8,128)S(1)}, f32[1,16,32]{2,1,0:T(8,128)S(1)}, u32[]{:S(2)}, u32[]{:S(2)}) collective-permute-start(f32[1,16,32]{2,1,0:T(8,128)S(1)} %get-tuple-element.166), channel_id=1, source_target_pairs={{0,4},{4,8},{8,12},{12,16},{16,20},{20,24},{24,28},{1,5},{5,9},{9,... | collective-permute-start | bytes 6152 | tf_op jit(solution)/shard_map/ppermute | solution.py:23
  289.5 5.9 %collective-permute-start.40 = (f32[1,16,32]{2,1,0:T(8,128)S(1)}, f32[1,16,32]{2,1,0:T(8,128)S(1)}, u32[]{:S(2)}, u32[]{:S(2)}) collective-permute-start(f32[1,16,32]{2,1,0:T(8,128)S(1)} %get-tuple-element.161), channel_id=1, source_target_pairs={{4,0},{8,4},{12,8},{16,12},{20,16},{24,20},{28,24},{5,1},{9,5},{13... | collective-permute-start | bytes 6152 | tf_op jit(solution)/shard_map/ppermute | solution.py:25
  291.4 6.4 %collective-permute-start.41 = (f32[1,16,32]{2,1,0:T(8,128)S(1)}, f32[1,16,32]{2,1,0:T(8,128)S(1)}, u32[]{:S(2)}, u32[]{:S(2)}) collective-permute-start(f32[1,16,32]{2,1,0:T(8,128)S(1)} %get-tuple-element.160), channel_id=1, source_target_pairs={{0,4},{4,8},{8,12},{12,16},{16,20},{20,24},{24,28},{1,5},{5,9},{9,... | collective-permute-start | bytes 6152 | tf_op jit(solution)/shard_map/ppermute | solution.py:23
  298.2 5.9 %collective-permute-start.42 = (f32[1,16,32]{2,1,0:T(8,128)S(1)}, f32[1,16,32]{2,1,0:T(8,128)S(1)}, u32[]{:S(2)}, u32[]{:S(2)}) collective-permute-start(f32[1,16,32]{2,1,0:T(8,128)S(1)} %get-tuple-element.159), channel_id=1, source_target_pairs={{4,0},{8,4},{12,8},{16,12},{20,16},{24,20},{28,24},{5,1},{9,5},{13... | collective-permute-start | bytes 6152 | tf_op jit(solution)/shard_map/ppermute | solution.py:25
  300.1 6.4 %collective-permute-start.43 = (f32[1,16,32]{2,1,0:T(8,128)S(1)}, f32[1,16,32]{2,1,0:T(8,128)S(1)}, u32[]{:S(2)}, u32[]{:S(2)}) collective-permute-start(f32[1,16,32]{2,1,0:T(8,128)S(1)} %get-tuple-element.158), channel_id=1, source_target_pairs={{0,4},{4,8},{8,12},{12,16},{16,20},{20,24},{24,28},{1,5},{5,9},{9,... | collective-permute-start | bytes 6152 | tf_op jit(solution)/shard_map/ppermute | solution.py:23
  307.0 5.9 %collective-permute-start.45 = (f32[1,1,8,64]{3,2,1,0:T(8,128)S(1)}, f32[1,1,8,64]{3,2,1,0:T(8,128)S(1)}, u32[]{:S(2)}, u32[]{:S(2)}) collective-permute-start(f32[1,1,8,64]{3,2,1,0:T(8,128)S(1)} %get-tuple-element.151), channel_id=1, source_target_pairs={{4,0},{8,4},{12,8},{16,12},{20,16},{24,20},{28,24},{5,1},{9,5},{13... | collective-permute-start | bytes 6152 | tf_op jit(solution)/shard_map/ppermute | solution.py:25
  309.0 6.4 %collective-permute-start.44 = (f32[1,1,8,64]{3,2,1,0:T(8,128)S(1)}, f32[1,1,8,64]{3,2,1,0:T(8,128)S(1)}, u32[]{:S(2)}, u32[]{:S(2)}) collective-permute-start(f32[1,1,8,64]{3,2,1,0:T(8,128)S(1)} %get-tuple-element.150), channel_id=1, source_target_pairs={{0,4},{4,8},{8,12},{12,16},{16,20},{20,24},{24,28},{1,5},{5,9},{9,... | collective-permute-start | bytes 6152 | tf_op jit(solution)/shard_map/ppermute | solution.py:23
  322.6 5.9 %collective-permute-start.49 = (f32[1,1,8,64]{3,2,1,0:T(8,128)S(1)}, f32[1,1,8,64]{3,2,1,0:T(8,128)S(1)}, u32[]{:S(2)}, u32[]{:S(2)}) collective-permute-start(f32[1,1,8,64]{3,2,1,0:T(8,128)S(1)} %get-tuple-element.149), channel_id=1, source_target_pairs={{4,0},{8,4},{12,8},{16,12},{20,16},{24,20},{28,24},{5,1},{9,5},{13... | collective-permute-start | bytes 6152 | tf_op jit(solution)/shard_map/ppermute | solution.py:25
  324.5 6.4 %collective-permute-start.48 = (f32[1,1,8,64]{3,2,1,0:T(8,128)S(1)}, f32[1,1,8,64]{3,2,1,0:T(8,128)S(1)}, u32[]{:S(2)}, u32[]{:S(2)}) collective-permute-start(f32[1,1,8,64]{3,2,1,0:T(8,128)S(1)} %get-tuple-element.148), channel_id=1, source_target_pairs={{0,4},{4,8},{8,12},{12,16},{16,20},{20,24},{24,28},{1,5},{5,9},{9,... | collective-permute-start | bytes 6152 | tf_op jit(solution)/shard_map/ppermute | solution.py:23
  338.2 5.9 %collective-permute-start.53 = (f32[1,1,8,64]{3,2,1,0:T(8,128)S(1)}, f32[1,1,8,64]{3,2,1,0:T(8,128)S(1)}, u32[]{:S(2)}, u32[]{:S(2)}) collective-permute-start(f32[1,1,8,64]{3,2,1,0:T(8,128)S(1)} %get-tuple-element.147), channel_id=1, source_target_pairs={{4,0},{8,4},{12,8},{16,12},{20,16},{24,20},{28,24},{5,1},{9,5},{13... | collective-permute-start | bytes 6152 | tf_op jit(solution)/shard_map/ppermute | solution.py:25
  340.1 6.4 %collective-permute-start.52 = (f32[1,1,8,64]{3,2,1,0:T(8,128)S(1)}, f32[1,1,8,64]{3,2,1,0:T(8,128)S(1)}, u32[]{:S(2)}, u32[]{:S(2)}) collective-permute-start(f32[1,1,8,64]{3,2,1,0:T(8,128)S(1)} %get-tuple-element.146), channel_id=1, source_target_pairs={{0,4},{4,8},{8,12},{12,16},{16,20},{20,24},{24,28},{1,5},{5,9},{9,... | collective-permute-start | bytes 6152 | tf_op jit(solution)/shard_map/ppermute | solution.py:23
  354.6 5.9 %collective-permute-start.57 = (f32[1,1,16,128]{3,2,1,0:T(8,128)S(1)}, f32[1,1,16,128]{3,2,1,0:T(8,128)S(1)}, u32[]{:S(2)}, u32[]{:S(2)}) collective-permute-start(f32[1,1,16,128]{3,2,1,0:T(8,128)S(1)} %get-tuple-element.103), channel_id=1, source_target_pairs={{4,0},{8,4},{12,8},{16,12},{20,16},{24,20},{28,24},{5,1},{9,5},{13... | collective-permute-start | bytes 24584 | tf_op jit(solution)/shard_map/ppermute | solution.py:25
  356.6 6.4 %collective-permute-start.56 = (f32[1,1,16,128]{3,2,1,0:T(8,128)S(1)}, f32[1,1,16,128]{3,2,1,0:T(8,128)S(1)}, u32[]{:S(2)}, u32[]{:S(2)}) collective-permute-start(f32[1,1,16,128]{3,2,1,0:T(8,128)S(1)} %get-tuple-element.102), channel_id=1, source_target_pairs={{0,4},{4,8},{8,12},{12,16},{16,20},{20,24},{24,28},{1,5},{5,9},{9,... | collective-permute-start | bytes 24584 | tf_op jit(solution)/shard_map/ppermute | solution.py:23
  370.4 5.9 %collective-permute-start.61 = (f32[1,1,16,128]{3,2,1,0:T(8,128)S(1)}, f32[1,1,16,128]{3,2,1,0:T(8,128)S(1)}, u32[]{:S(2)}, u32[]{:S(2)}) collective-permute-start(f32[1,1,16,128]{3,2,1,0:T(8,128)S(1)} %get-tuple-element.101), channel_id=1, source_target_pairs={{4,0},{8,4},{12,8},{16,12},{20,16},{24,20},{28,24},{5,1},{9,5},{13... | collective-permute-start | bytes 24584 | tf_op jit(solution)/shard_map/ppermute | solution.py:25
  372.4 6.4 %collective-permute-start.60 = (f32[1,1,16,128]{3,2,1,0:T(8,128)S(1)}, f32[1,1,16,128]{3,2,1,0:T(8,128)S(1)}, u32[]{:S(2)}, u32[]{:S(2)}) collective-permute-start(f32[1,1,16,128]{3,2,1,0:T(8,128)S(1)} %get-tuple-element.100), channel_id=1, source_target_pairs={{0,4},{4,8},{8,12},{12,16},{16,20},{20,24},{24,28},{1,5},{5,9},{9,... | collective-permute-start | bytes 24584 | tf_op jit(solution)/shard_map/ppermute | solution.py:23
  386.3 5.9 %collective-permute-start.65 = (f32[1,1,16,128]{3,2,1,0:T(8,128)S(1)}, f32[1,1,16,128]{3,2,1,0:T(8,128)S(1)}, u32[]{:S(2)}, u32[]{:S(2)}) collective-permute-start(f32[1,1,16,128]{3,2,1,0:T(8,128)S(1)} %get-tuple-element.99), channel_id=1, source_target_pairs={{4,0},{8,4},{12,8},{16,12},{20,16},{24,20},{28,24},{5,1},{9,5},{13... | collective-permute-start | bytes 24584 | tf_op jit(solution)/shard_map/ppermute | solution.py:25
  388.2 6.4 %collective-permute-start.64 = (f32[1,1,16,128]{3,2,1,0:T(8,128)S(1)}, f32[1,1,16,128]{3,2,1,0:T(8,128)S(1)}, u32[]{:S(2)}, u32[]{:S(2)}) collective-permute-start(f32[1,1,16,128]{3,2,1,0:T(8,128)S(1)} %get-tuple-element.98), channel_id=1, source_target_pairs={{0,4},{4,8},{8,12},{12,16},{16,20},{20,24},{24,28},{1,5},{5,9},{9,... | collective-permute-start | bytes 24584 | tf_op jit(solution)/shard_map/ppermute | solution.py:23
  (22 other events, 116.4 us)
where the time goes:
time: 405 us; the launch traced here: 403 us
  starting transfers between devices  181 us (45%)
  waiting for transfers between devices  85.1 us (21%)
  other arithmetic  69.4 us (17%)
  local copies, waits for them, and re-layouts  49.5 us (12%)
  blocking collectives  15.9 us (4%)
    ppermute x34, starting transfers between devices, padded_2(): lax.ppermute(tail, axis, [(i, (i + 1) % count) for i in range(ends)])  105 us
    ppermute x34, waiting for transfers between devices, padded_2(): lax.ppermute(tail, axis, [(i, (i + 1) % count) for i in range(ends)])  83 us
    ppermute x34, starting transfers between devices, padded_2(): lax.ppermute(head, axis, [((i + 1) % count, i) for i in range(ends)])  76.4 us
    reduce_sum x4, other arithmetic, coarsen(): return jnp.mean(split, axis=(-5, -3, -1))  36.5 us
    concatenate x1, local copies, waits for them, and re-layouts, padded_2(): jnp.concatenate([lax.ppermute(tail, axis, [(i, (i + 1) % count) for i in...  18.2 us
    another operation x3, other arithmetic, local_fields(): return jnp.stack([fields[0], fields[1], fields[2], storage])  16.5 us
    reshape x2, local copies, waits for them, and re-layouts, coarsen(): values.reshape(lead + (size_x // 2, 2, size_y // 2, 2, size_z // 2, 2))  10.9 us
    all_gather x1, blocking collectives, local(): lax.all_gather(narrow, 'gy', axis=2, tiled=True)  10.7 us
  transfers between devices with their start and end apart: 68, of which 33 were waited for; matrix products, arithmetic and copies ran while one was open for 15% of the time, Pallas kernels for 0%

commit v1 on v0

--- a/solution.py
+++ b/solution.py
@@ -10,6 +10,28 @@
 cheb_half = 0.9
 cheb_ratio = cheb_centre / cheb_half
 jacobi_weight = 0.8
+
+
+def in_order(blocks, dim):
+    blocks = jnp.moveaxis(blocks, 0, dim)
+    shape = blocks.shape
+    return blocks.reshape(*shape[:dim], shape[dim] * shape[dim + 1], *shape[dim + 2 :])
+
+
+def gather_around(x, axis, dim):
+    size = lax.axis_size(axis)
+    pairs = [(i, (i + 1) % size) for i in range(size)]
+    back = [(b, a) for a, b in pairs]
+    lower, upper = ([], [])
+    for hop in range(size - 1):
+        if hop % 2 == 0:
+            lower.append(lax.ppermute(lower[-1] if lower else x, axis, pairs))
+        else:
+            upper.append(lax.ppermute(upper[-1] if upper else x, axis, back))
+    blocks = jnp.stack([*lower[::-1], x, *upper])
+    shift = lax.axis_index(axis) - len(lower)
+    blocks = blocks[(jnp.arange(size) - shift) % size]
+    return in_order(blocks, dim)
 
 
 def padded_2(cells, sides, width):
@@ -172,7 +194,7 @@
     narrow = coarse_coeffs[:, :, 1:-1]
     group_source, group_coeffs = (
         lax.all_gather(coarse_source, "gy", axis=1, tiled=True),
-        lax.all_gather(narrow, "gy", axis=2, tiled=True),
+        gather_around(narrow, "gy", 2),
     )
     line_total = jnp.sum(group_source, axis=1)
     line_store = jnp.sum(group_coeffs[3, 1:-1], axis=1)

time: 405 us -> 393 us (0.970)
  blocking collectives: 15.9 us -> 5.19 us
    all_gather x1 -> x0, blocking collectives: 10.7 us -> none  [local(): lax.all_gather(narrow, 'gy', axis=2, tiled=True)]
    ppermute x34, starting transfers between devices: 76.4 us -> 71.1 us  [padded_2(): lax.ppermute(head, axis, [((i + 1) % count, i) for i in range(ends)])]
  transfers between devices with their start and end apart: 68 -> 71, of which waited for: 33 -> 34; matrix products, arithmetic and copies ran while one was open for 15% -> 15% of each run, Pallas kernels for 0% -> 0%
where the time goes in v1:
time: 393 us; the launch traced here: 390 us
  starting transfers between devices  181 us (46%)
  waiting for transfers between devices  86.3 us (22%)
  other arithmetic  68.6 us (17%)
  local copies, waits for them, and re-layouts  47.8 us (12%)
  blocking collectives  5.19 us (1%)
    ppermute x34, starting transfers between devices, padded_2(): lax.ppermute(tail, axis, [(i, (i + 1) % count) for i in range(ends)])  108 us
    ppermute x34, waiting for transfers between devices, padded_2(): lax.ppermute(tail, axis, [(i, (i + 1) % count) for i in range(ends)])  84.2 us
    ppermute x34, starting transfers between devices, padded_2(): lax.ppermute(head, axis, [((i + 1) % count, i) for i in range(ends)])  71.1 us
    reduce_sum x4, other arithmetic, coarsen(): return jnp.mean(split, axis=(-5, -3, -1))  36.6 us
    concatenate x1, local copies, waits for them, and re-layouts, padded_2(): jnp.concatenate([lax.ppermute(tail, axis, [(i, (i + 1) % count) for i in...  17.9 us
    another operation x3, other arithmetic, local_fields(): return jnp.stack([fields[0], fields[1], fields[2], storage])  16.1 us
    reshape x2, local copies, waits for them, and re-layouts, coarsen(): values.reshape(lead + (size_x // 2, 2, size_y // 2, 2, size_z // 2, 2))  10.8 us
    mul x1, other arithmetic, local_fields(): storage_scale * (1.0 + fields[3] * jnp.exp((fields[4] - 1.0) * jnp.log(co...  10.4 us
  transfers between devices with their start and end apart: 71, of which 34 were waited for; matrix products, arithmetic and copies ran while one was open for 15% of the time, Pallas kernels for 0%

profile of v1, /device:TPU:26, one launch (start us, length us, event | category | flops | bytes accessed | tf_op | source)
XLA Modules:
  0.0 390.0 jit_solution(3949715331509523406)
XLA Ops:
  5.5 6.0 %add_bitcast_fusion.3 = (f32[1,16,16,128]{3,2,1,0:T(8,128)S(1)}, pred[16,16,128]{2,1,0:T(8,128)(4,1)S(1)}, pred[16,16,128]{2,1,0:T(8,128)(4,1)S(1)}, pred[16,16,...) fusion(f32[]{:T(128)} %bitcast.23, f32[]{:T(128)} %bitcast.22, ...), kind=kLoop, calls=%fused_computation.161 | loop fusion | flops 753664 | bytes 524320 | tf_op jit(solution)/shard_map/stack | solution.py:175
  11.5 5.1 %add_bitcast_fusion.1 = f32[1,16,16,128]{3,2,1,0:T(8,128)S(1)} fusion(pred[16,16,128]{2,1,0:T(8,128)(4,1)S(1)} %get-tuple-element.44, pred[16,16,128]{2,1,0:T(8,128)(4,1)S(1)} %get-tuple-element.43, pred[16,16,128]{2,1,0:T(8,128)(4,1)S(1)} %get-tuple-element.42, pred[16,16,128]{2,1,0:T(8,128)(4,1)S(1)} %get-tuple-element.41, ...), kind=kLoop, calls=%fused_computation.159 | loop fusion | flops 491520 | bytes 393248 | tf_op jit(solution)/shard_map/stack | solution.py:175
  16.6 5.1 %add_bitcast_fusion.2 = f32[1,16,16,128]{3,2,1,0:T(8,128)S(1)} fusion(pred[16,16,128]{2,1,0:T(8,128)(4,1)S(1)} %get-tuple-element.44, pred[16,16,128]{2,1,0:T(8,128)(4,1)S(1)} %get-tuple-element.43, pred[16,16,128]{2,1,0:T(8,128)(4,1)S(1)} %get-tuple-element.42, pred[16,16,128]{2,1,0:T(8,128)(4,1)S(1)} %get-tuple-element.41, ...), kind=kLoop, calls=%fused_computation.160 | loop fusion | flops 491520 | bytes 393248 | tf_op jit(solution)/shard_map/stack | solution.py:175
  21.7 10.4 %add_multiply_fusion = f32[16,16,128]{2,1,0:T(8,128)S(1)} fusion(f32[16,16,128]{2,1,0:T(8,128)S(1)} %copy-done.1, pred[16,16,128]{2,1,0:T(8,128)(4,1)S(1)} %get-tuple-element.44, pred[16,16,128]{2,1,0:T(8,128)(4,1)S(1)} %get-tuple-element.43, pred[16,16,128]{2,1,0:T(8,128)(4,1)S(1)} %get-tuple-element.42, pred[16,16,128]{2,1,0:T(8,128)(4,1)S(1)} %get-tuple-element.41, ...), kind=kLoop, calls=%fused_computation.162 | loop fusion | flops 1146880 | bytes 524352 | tf_op jit(solution)/shard_map/mul | solution.py:174
  32.1 3.3 collective-permute-start.1
  39.2 4.0 %collective-permute-done = f32[4,4,16,128]{3,2,1,0:T(8,128)S(1)} collective-permute-done((f32[4,4,16,128]{3,2,1,0:T(8,128)S(1)}, f32[4,4,16,128]{3,2,1,0:T(8,128)S(1)}, u32[]{:S(2)}, u32[]{:S(2)}) %collective-permute-start) | collective-permute-done | bytes 131104 | tf_op jit(solution)/shard_map/ppermute | solution.py:45
  48.4 3.8 collective-permute-done.2
  53.6 3.2 collective-permute-start.5
  56.8 2.6 collective-permute-start.4
  59.4 3.8 collective-permute-done.4
  72.6 3.9 %collective-permute-start.8 = (f32[1,1,16,128]{3,2,1,0:T(8,128)S(1)}, f32[1,1,16,128]{3,2,1,0:T(8,128)S(1)}, u32[]{:S(2)}, u32[]{:S(2)}) collective-permute-start(f32[1,1,16,128]{3,2,1,0:T(8,128)S(1)} %get-tuple-element.106), channel_id=1, source_target_pairs={{0,4},{4,8},{8,12},{12,16},{16,20},{20,24},{24,28},{1,5},{5,9},{9,... | collective-permute-start | bytes 24584 | tf_op jit(solution)/shard_map/ppermute | solution.py:45
  76.5 17.9 %copy.584 = f32[4,24,24,128]{0,3,2,1:T(8,128)} copy(f32[4,24,24,128]{3,2,1,0:T(8,128)S(1)} %pad_maximum_fusion) | data formatting | bytes 2359296 | tf_op jit(solution)/shard_map/concatenate | solution.py:43
  94.5 27.0 %reduce_sum.55 = f32[4,12,12,64]{0,3,2,1:T(8,128)} reduce(f32[4,12,2,12,2,64,2]{0,6,5,4,3,2,1:T(2,128)} %bitcast.194, f32[]{:T(128)} %constant.28.clone.1), dimensions={2,4,6}, to_apply=%region_1.2 | reduce | flops 258048 | bytes 1327108 | tf_op jit(solution)/shard_map/reduce_sum | solution.py:107
  121.5 3.7 copy.585
  132.7 2.8 collective-permute-start.13
  135.5 3.0 collective-permute-start.12
  138.6 3.4 collective-permute-done.12
  143.9 2.6 collective-permute-start.14
  146.6 3.1 copy.597
  149.7 5.3 %reduce_sum.58 = f32[4,6,6,32]{0,3,2,1:T(8,128)S(1)} reduce(f32[4,6,2,6,2,32,2]{0,6,5,4,3,2,1:T(2,128)} %bitcast.195, f32[]{:T(128)} %constant.28.clone.1), dimensions={2,4,6}, to_apply=%region_4.5 | reduce | flops 32256 | bytes 165892 | tf_op jit(solution)/shard_map/reduce_sum | solution.py:107
  155.8 9.8 %reshape.108 = f32[8,2,8,2,64,2]{5,4,3,2,1,0:T(8,128)} reshape(f32[16,16,128]{2,1,0:T(8,128)S(1)} %fusion.41) | data formatting | bytes 262144 | tf_op jit(solution)/shard_map/reshape | solution.py:106
  165.5 4.0 %reduce_sum.54 = f32[8,8,64]{2,1,0:T(8,128)S(1)} reduce(f32[8,2,8,2,64,2]{5,4,3,2,1,0:T(8,128)} %reshape.108, f32[]{:T(128)} %constant.28.clone.1), dimensions={1,3,5}, to_apply=%region_0.1 | reduce | flops 28672 | bytes 147460 | tf_op jit(solution)/shard_map/reduce_sum | solution.py:107
  171.7 3.8 collective-permute-start.16
  185.3 2.8 collective-permute-start.21
  188.1 3.0 collective-permute-start.20
  192.0 2.6 collective-permute-done.20
  203.8 3.8 collective-permute-start.24
  218.7 5.2 %all_gather.3 = f32[4,16,32]{2,0,1:T(4,128)S(1)} all-gather(f32[4,4,32]{2,0,1:T(4,128)S(1)} %copy.595), channel_id=1, replica_groups=mesh['gx'=8,'gy'=4] {'gy'}, dimensions={1}, use_global_device_ids=true | all-gather | bytes 10240 | tf_op jit(solution)/shard_map/all_gather | solution.py:196
  224.0 2.8 collective-permute-start.31
  226.8 3.0 collective-permute-start.32
  230.0 3.2 collective-permute-done.32
  235.7 3.8 collective-permute-start.34
  244.4 3.8 collective-permute-start.36
  248.2 2.6 collective-permute-done.36
  253.0 3.9 %collective-permute-start.38 = (f32[1,16,32]{2,1,0:T(8,128)S(1)}, f32[1,16,32]{2,1,0:T(8,128)S(1)}, u32[]{:S(2)}, u32[]{:S(2)}) collective-permute-start(f32[1,16,32]{2,1,0:T(8,128)S(1)} %get-tuple-element.180), channel_id=1, source_target_pairs={{0,4},{4,8},{8,12},{12,16},{16,20},{20,24},{24,28},{1,5},{5,9},{9,... | collective-permute-start | bytes 6152 | tf_op jit(solution)/shard_map/ppermute | solution.py:45
  261.6 3.9 %collective-permute-start.40 = (f32[1,16,32]{2,1,0:T(8,128)S(1)}, f32[1,16,32]{2,1,0:T(8,128)S(1)}, u32[]{:S(2)}, u32[]{:S(2)}) collective-permute-start(f32[1,16,32]{2,1,0:T(8,128)S(1)} %get-tuple-element.174), channel_id=1, source_target_pairs={{0,4},{4,8},{8,12},{12,16},{16,20},{20,24},{24,28},{1,5},{5,9},{9,... | collective-permute-start | bytes 6152 | tf_op jit(solution)/shard_map/ppermute | solution.py:45
  270.1 3.9 %collective-permute-start.42 = (f32[1,16,32]{2,1,0:T(8,128)S(1)}, f32[1,16,32]{2,1,0:T(8,128)S(1)}, u32[]{:S(2)}, u32[]{:S(2)}) collective-permute-start(f32[1,16,32]{2,1,0:T(8,128)S(1)} %get-tuple-element.168), channel_id=1, source_target_pairs={{0,4},{4,8},{8,12},{12,16},{16,20},{20,24},{24,28},{1,5},{5,9},{9,... | collective-permute-start | bytes 6152 | tf_op jit(solution)/shard_map/ppermute | solution.py:45
  278.7 3.9 %collective-permute-start.44 = (f32[1,16,32]{2,1,0:T(8,128)S(1)}, f32[1,16,32]{2,1,0:T(8,128)S(1)}, u32[]{:S(2)}, u32[]{:S(2)}) collective-permute-start(f32[1,16,32]{2,1,0:T(8,128)S(1)} %get-tuple-element.162), channel_id=1, source_target_pairs={{0,4},{4,8},{8,12},{12,16},{16,20},{20,24},{24,28},{1,5},{5,9},{9,... | collective-permute-start | bytes 6152 | tf_op jit(solution)/shard_map/ppermute | solution.py:45
  287.4 3.9 %collective-permute-start.46 = (f32[1,16,32]{2,1,0:T(8,128)S(1)}, f32[1,16,32]{2,1,0:T(8,128)S(1)}, u32[]{:S(2)}, u32[]{:S(2)}) collective-permute-start(f32[1,16,32]{2,1,0:T(8,128)S(1)} %get-tuple-element.160), channel_id=1, source_target_pairs={{0,4},{4,8},{8,12},{12,16},{16,20},{20,24},{24,28},{1,5},{5,9},{9,... | collective-permute-start | bytes 6152 | tf_op jit(solution)/shard_map/ppermute | solution.py:45
  296.2 3.9 %collective-permute-start.47 = (f32[1,1,8,64]{3,2,1,0:T(8,128)S(1)}, f32[1,1,8,64]{3,2,1,0:T(8,128)S(1)}, u32[]{:S(2)}, u32[]{:S(2)}) collective-permute-start(f32[1,1,8,64]{3,2,1,0:T(8,128)S(1)} %get-tuple-element.152), channel_id=1, source_target_pairs={{0,4},{4,8},{8,12},{12,16},{16,20},{20,24},{24,28},{1,5},{5,9},{9,... | collective-permute-start | bytes 6152 | tf_op jit(solution)/shard_map/ppermute | solution.py:45
  304.6 2.6 collective-permute-start.49
  311.8 3.9 %collective-permute-start.51 = (f32[1,1,8,64]{3,2,1,0:T(8,128)S(1)}, f32[1,1,8,64]{3,2,1,0:T(8,128)S(1)}, u32[]{:S(2)}, u32[]{:S(2)}) collective-permute-start(f32[1,1,8,64]{3,2,1,0:T(8,128)S(1)} %get-tuple-element.150), channel_id=1, source_target_pairs={{0,4},{4,8},{8,12},{12,16},{16,20},{20,24},{24,28},{1,5},{5,9},{9,... | collective-permute-start | bytes 6152 | tf_op jit(solution)/shard_map/ppermute | solution.py:45
  327.4 3.9 collective-permute-start.55
  343.9 3.9 %collective-permute-start.59 = (f32[1,1,16,128]{3,2,1,0:T(8,128)S(1)}, f32[1,1,16,128]{3,2,1,0:T(8,128)S(1)}, u32[]{:S(2)}, u32[]{:S(2)}) collective-permute-start(f32[1,1,16,128]{3,2,1,0:T(8,128)S(1)} %get-tuple-element.102), channel_id=1, source_target_pairs={{0,4},{4,8},{8,12},{12,16},{16,20},{20,24},{24,28},{1,5},{5,9},{9,... | collective-permute-start | bytes 24584 | tf_op jit(solution)/shard_map/ppermute | solution.py:45
  354.7 2.6 collective-permute-done.61
  359.7 3.9 %collective-permute-start.63 = (f32[1,1,16,128]{3,2,1,0:T(8,128)S(1)}, f32[1,1,16,128]{3,2,1,0:T(8,128)S(1)}, u32[]{:S(2)}, u32[]{:S(2)}) collective-permute-start(f32[1,1,16,128]{3,2,1,0:T(8,128)S(1)} %get-tuple-element.100), channel_id=1, source_target_pairs={{0,4},{4,8},{8,12},{12,16},{16,20},{20,24},{24,28},{1,5},{5,9},{9,... | collective-permute-start | bytes 24584 | tf_op jit(solution)/shard_map/ppermute | solution.py:45
  370.5 2.6 collective-permute-done.65
  375.5 3.9 %collective-permute-start.67 = (f32[1,1,16,128]{3,2,1,0:T(8,128)S(1)}, f32[1,1,16,128]{3,2,1,0:T(8,128)S(1)}, u32[]{:S(2)}, u32[]{:S(2)}) collective-permute-start(f32[1,1,16,128]{3,2,1,0:T(8,128)S(1)} %get-tuple-element.98), channel_id=1, source_target_pairs={{0,4},{4,8},{8,12},{12,16},{16,20},{20,24},{24,28},{1,5},{5,9},{9,... | collective-permute-start | bytes 24584 | tf_op jit(solution)/shard_map/ppermute | solution.py:45
  (291 shorter events, 163.3 us)
Async XLA Ops:
  32.1 7.1 %collective-permute-start.1 = (f32[4,4,16,128]{3,2,1,0:T(8,128)S(1)}, f32[4,4,16,128]{3,2,1,0:T(8,128)S(1)}, u32[]{:S(2)}, u32[]{:S(2)}) collective-permute-start(f32[4,4,16,128]{3,2,1,0:T(8,128)S(1)} %get-tuple-element.51), channel_id=1, source_target_pairs={{4,0},{8,4},{12,8},{16,12},{20,16},{24,20},{28,24},{5,1},{9,5},{13... | collective-permute-start | bytes 393224 | tf_op jit(solution)/shard_map/ppermute | solution.py:47
  35.4 7.8 %collective-permute-start = (f32[4,4,16,128]{3,2,1,0:T(8,128)S(1)}, f32[4,4,16,128]{3,2,1,0:T(8,128)S(1)}, u32[]{:S(2)}, u32[]{:S(2)}) collective-permute-start(f32[4,4,16,128]{3,2,1,0:T(8,128)S(1)} %get-tuple-element.50), channel_id=1, source_target_pairs={{0,4},{4,8},{8,12},{12,16},{16,20},{20,24},{24,28},{1,5},{5,9},{9,... | collective-permute-start | bytes 393224 | tf_op jit(solution)/shard_map/ppermute | solution.py:45
  45.2 7.0 %collective-permute-start.2 = (f32[4,24,4,128]{3,1,2,0:T(8,128)S(1)}, f32[4,24,4,128]{3,1,2,0:T(8,128)S(1)}, u32[]{:S(2)}, u32[]{:S(2)}) collective-permute-start(f32[4,24,4,128]{3,1,2,0:T(8,128)S(1)} %copy.630), channel_id=1, source_target_pairs={{0,1},{1,2},{2,3},{4,5},{5,6},{6,7},{8,9},{9,10},{10,11},{12,13},{... | collective-permute-start | bytes 589832 | tf_op jit(solution)/shard_map/ppermute | solution.py:45
  53.6 5.9 %collective-permute-start.5 = (f32[1,1,16,128]{3,2,1,0:T(8,128)S(1)}, f32[1,1,16,128]{3,2,1,0:T(8,128)S(1)}, u32[]{:S(2)}, u32[]{:S(2)}) collective-permute-start(f32[1,1,16,128]{3,2,1,0:T(8,128)S(1)} %get-tuple-element.109), channel_id=1, source_target_pairs={{4,0},{8,4},{12,8},{16,12},{20,16},{24,20},{28,24},{5,1},{9,5},{13... | collective-permute-start | bytes 24584 | tf_op jit(solution)/shard_map/ppermute | solution.py:47
  56.8 6.4 %collective-permute-start.4 = (f32[1,1,16,128]{3,2,1,0:T(8,128)S(1)}, f32[1,1,16,128]{3,2,1,0:T(8,128)S(1)}, u32[]{:S(2)}, u32[]{:S(2)}) collective-permute-start(f32[1,1,16,128]{3,2,1,0:T(8,128)S(1)} %get-tuple-element.108), channel_id=1, source_target_pairs={{0,4},{4,8},{8,12},{12,16},{16,20},{20,24},{24,28},{1,5},{5,9},{9,... | collective-permute-start | bytes 24584 | tf_op jit(solution)/shard_map/ppermute | solution.py:45
  70.7 54.6 %collective-permute-start.9 = (f32[1,1,16,128]{3,2,1,0:T(8,128)S(1)}, f32[1,1,16,128]{3,2,1,0:T(8,128)S(1)}, u32[]{:S(2)}, u32[]{:S(2)}) collective-permute-start(f32[1,1,16,128]{3,2,1,0:T(8,128)S(1)} %get-tuple-element.107), channel_id=1, source_target_pairs={{4,0},{8,4},{12,8},{16,12},{20,16},{24,20},{28,24},{5,1},{9,5},{13... | collective-permute-start | bytes 24584 | tf_op jit(solution)/shard_map/ppermute | solution.py:47
  72.6 52.7 %collective-permute-start.8 = (f32[1,1,16,128]{3,2,1,0:T(8,128)S(1)}, f32[1,1,16,128]{3,2,1,0:T(8,128)S(1)}, u32[]{:S(2)}, u32[]{:S(2)}) collective-permute-start(f32[1,1,16,128]{3,2,1,0:T(8,128)S(1)} %get-tuple-element.106), channel_id=1, source_target_pairs={{0,4},{4,8},{8,12},{12,16},{16,20},{20,24},{24,28},{1,5},{5,9},{9,... | collective-permute-start | bytes 24584 | tf_op jit(solution)/shard_map/ppermute | solution.py:45
  132.7 5.9 %collective-permute-start.13 = (f32[1,1,16,128]{3,2,1,0:T(8,128)S(1)}, f32[1,1,16,128]{3,2,1,0:T(8,128)S(1)}, u32[]{:S(2)}, u32[]{:S(2)}) collective-permute-start(f32[1,1,16,128]{3,2,1,0:T(8,128)S(1)} %get-tuple-element.105), channel_id=1, source_target_pairs={{4,0},{8,4},{12,8},{16,12},{20,16},{24,20},{28,24},{5,1},{9,5},{13... | collective-permute-start | bytes 24584 | tf_op jit(solution)/shard_map/ppermute | solution.py:47
  135.5 6.4 %collective-permute-start.12 = (f32[1,1,16,128]{3,2,1,0:T(8,128)S(1)}, f32[1,1,16,128]{3,2,1,0:T(8,128)S(1)}, u32[]{:S(2)}, u32[]{:S(2)}) collective-permute-start(f32[1,1,16,128]{3,2,1,0:T(8,128)S(1)} %get-tuple-element.104), channel_id=1, source_target_pairs={{0,4},{4,8},{8,12},{12,16},{16,20},{20,24},{24,28},{1,5},{5,9},{9,... | collective-permute-start | bytes 24584 | tf_op jit(solution)/shard_map/ppermute | solution.py:45
  142.0 13.3 %collective-permute-start.15 = (f32[1,18,1,128]{3,2,1,0:T(1,128)S(1)}, f32[1,18,1,128]{3,2,1,0:T(1,128)S(1)}, u32[]{:S(2)}, u32[]{:S(2)}) collective-permute-start(f32[1,18,1,128]{3,2,1,0:T(1,128)S(1)} %get-tuple-element.93), channel_id=1, source_target_pairs={{1,0},{2,1},{3,2},{5,4},{6,5},{7,6},{9,8},{10,9},{11,10},{13,12},{... | collective-permute-start | bytes 27656 | tf_op jit(solution)/shard_map/ppermute | solution.py:47
  143.9 11.4 %collective-permute-start.14 = (f32[1,18,1,128]{3,2,1,0:T(1,128)S(1)}, f32[1,18,1,128]{3,2,1,0:T(1,128)S(1)}, u32[]{:S(2)}, u32[]{:S(2)}) collective-permute-start(f32[1,18,1,128]{3,2,1,0:T(1,128)S(1)} %get-tuple-element.92), channel_id=1, source_target_pairs={{0,1},{1,2},{2,3},{4,5},{5,6},{6,7},{8,9},{9,10},{10,11},{12,13},{... | collective-permute-start | bytes 27656 | tf_op jit(solution)/shard_map/ppermute | solution.py:45
  169.7 5.9 %collective-permute-start.17 = (f32[1,1,8,64]{3,2,1,0:T(8,128)S(1)}, f32[1,1,8,64]{3,2,1,0:T(8,128)S(1)}, u32[]{:S(2)}, u32[]{:S(2)}) collective-permute-start(f32[1,1,8,64]{3,2,1,0:T(8,128)S(1)} %get-tuple-element.203), channel_id=1, source_target_pairs={{4,0},{8,4},{12,8},{16,12},{20,16},{24,20},{28,24},{5,1},{9,5},{13... | collective-permute-start | bytes 6152 | tf_op jit(solution)/shard_map/ppermute | solution.py:47
  171.7 6.4 %collective-permute-start.16 = (f32[1,1,8,64]{3,2,1,0:T(8,128)S(1)}, f32[1,1,8,64]{3,2,1,0:T(8,128)S(1)}, u32[]{:S(2)}, u32[]{:S(2)}) collective-permute-start(f32[1,1,8,64]{3,2,1,0:T(8,128)S(1)} %get-tuple-element.202), channel_id=1, source_target_pairs={{0,4},{4,8},{8,12},{12,16},{16,20},{20,24},{24,28},{1,5},{5,9},{9,... | collective-permute-start | bytes 6152 | tf_op jit(solution)/shard_map/ppermute | solution.py:45
  175.5 8.2 %collective-permute-start.28 = (f32[4,6,4,32]{3,2,1,0:T(4,128)S(1)}, f32[4,6,4,32]{3,2,1,0:T(4,128)S(1)}, u32[]{:S(2)}, u32[]{:S(2)}) collective-permute-start(f32[4,6,4,32]{3,2,1,0:T(4,128)S(1)} %get-tuple-element.135), channel_id=1, source_target_pairs={{0,1},{1,2},{2,3},{3,0},{4,5},{5,6},{6,7},{7,4},{8,9},{9,10},{10,1... | collective-permute-start | bytes 36872 | tf_op jit(solution)/shard_map/ppermute | solution.py:28
  182.4 8.7 %collective-permute-start.30 = (f32[4,6,4,32]{3,2,1,0:T(4,128)S(1)}, f32[4,6,4,32]{3,2,1,0:T(4,128)S(1)}, u32[]{:S(2)}, u32[]{:S(2)}) collective-permute-start(f32[4,6,4,32]{3,2,1,0:T(4,128)S(1)} %get-tuple-element.135), channel_id=1, source_target_pairs={{1,0},{2,1},{3,2},{0,3},{5,4},{6,5},{7,6},{4,7},{9,8},{10,9},{11,1... | collective-permute-start | bytes 36872 | tf_op jit(solution)/shard_map/ppermute | solution.py:30
  183.8 7.4 %collective-permute-start.29 = (f32[4,6,4,32]{3,2,1,0:T(4,128)S(1)}, f32[4,6,4,32]{3,2,1,0:T(4,128)S(1)}, u32[]{:S(2)}, u32[]{:S(2)}) collective-permute-start(f32[4,6,4,32]{3,2,1,0:T(4,128)S(1)} %collective-permute-done.28), channel_id=1, source_target_pairs={{0,1},{1,2},{2,3},{3,0},{4,5},{5,6},{6,7},{7,4},{8,9},{9,10},{10,1... | collective-permute-start | bytes 36872 | tf_op jit(solution)/shard_map/ppermute | solution.py:28
  185.3 6.7 %collective-permute-start.21 = (f32[1,1,8,64]{3,2,1,0:T(8,128)S(1)}, f32[1,1,8,64]{3,2,1,0:T(8,128)S(1)}, u32[]{:S(2)}, u32[]{:S(2)}) collective-permute-start(f32[1,1,8,64]{3,2,1,0:T(8,128)S(1)} %get-tuple-element.201), channel_id=1, source_target_pairs={{4,0},{8,4},{12,8},{16,12},{20,16},{24,20},{28,24},{5,1},{9,5},{13... | collective-permute-start | bytes 6152 | tf_op jit(solution)/shard_map/ppermute | solution.py:47
  188.1 6.4 %collective-permute-start.20 = (f32[1,1,8,64]{3,2,1,0:T(8,128)S(1)}, f32[1,1,8,64]{3,2,1,0:T(8,128)S(1)}, u32[]{:S(2)}, u32[]{:S(2)}) collective-permute-start(f32[1,1,8,64]{3,2,1,0:T(8,128)S(1)} %get-tuple-element.200), channel_id=1, source_target_pairs={{0,4},{4,8},{8,12},{12,16},{16,20},{20,24},{24,28},{1,5},{5,9},{9,... | collective-permute-start | bytes 6152 | tf_op jit(solution)/shard_map/ppermute | solution.py:45
  201.8 5.9 %collective-permute-start.25 = (f32[1,1,8,64]{3,2,1,0:T(8,128)S(1)}, f32[1,1,8,64]{3,2,1,0:T(8,128)S(1)}, u32[]{:S(2)}, u32[]{:S(2)}) collective-permute-start(f32[1,1,8,64]{3,2,1,0:T(8,128)S(1)} %get-tuple-element.199), channel_id=1, source_target_pairs={{4,0},{8,4},{12,8},{16,12},{20,16},{24,20},{28,24},{5,1},{9,5},{13... | collective-permute-start | bytes 6152 | tf_op jit(solution)/shard_map/ppermute | solution.py:47
  203.8 6.4 %collective-permute-start.24 = (f32[1,1,8,64]{3,2,1,0:T(8,128)S(1)}, f32[1,1,8,64]{3,2,1,0:T(8,128)S(1)}, u32[]{:S(2)}, u32[]{:S(2)}) collective-permute-start(f32[1,1,8,64]{3,2,1,0:T(8,128)S(1)} %get-tuple-element.198), channel_id=1, source_target_pairs={{0,4},{4,8},{8,12},{12,16},{16,20},{20,24},{24,28},{1,5},{5,9},{9,... | collective-permute-start | bytes 6152 | tf_op jit(solution)/shard_map/ppermute | solution.py:45
  224.0 6.0 %collective-permute-start.31 = (f32[1,16,32]{2,1,0:T(8,128)S(1)}, f32[1,16,32]{2,1,0:T(8,128)S(1)}, u32[]{:S(2)}, u32[]{:S(2)}) collective-permute-start(f32[1,16,32]{2,1,0:T(8,128)S(1)} %broadcast_in_dim.285), channel_id=1, source_target_pairs={{4,0},{8,4},{12,8},{16,12},{20,16},{24,20},{28,24},{5,1},{9,5},{13... | collective-permute-start | bytes 6152 | tf_op jit(solution)/shard_map/ppermute | solution.py:47
  226.8 6.4 %collective-permute-start.32 = (f32[1,16,32]{2,1,0:T(8,128)S(1)}, f32[1,16,32]{2,1,0:T(8,128)S(1)}, u32[]{:S(2)}, u32[]{:S(2)}) collective-permute-start(f32[1,16,32]{2,1,0:T(8,128)S(1)} %broadcast_in_dim.286), channel_id=1, source_target_pairs={{0,4},{4,8},{8,12},{12,16},{16,20},{20,24},{24,28},{1,5},{5,9},{9,... | collective-permute-start | bytes 6152 | tf_op jit(solution)/shard_map/ppermute | solution.py:45
  233.7 5.9 %collective-permute-start.33 = (f32[1,16,32]{2,1,0:T(8,128)S(1)}, f32[1,16,32]{2,1,0:T(8,128)S(1)}, u32[]{:S(2)}, u32[]{:S(2)}) collective-permute-start(f32[1,16,32]{2,1,0:T(8,128)S(1)} %get-tuple-element.193), channel_id=1, source_target_pairs={{4,0},{8,4},{12,8},{16,12},{20,16},{24,20},{28,24},{5,1},{9,5},{13... | collective-permute-start | bytes 6152 | tf_op jit(solution)/shard_map/ppermute | solution.py:47
  235.7 6.4 %collective-permute-start.34 = (f32[1,16,32]{2,1,0:T(8,128)S(1)}, f32[1,16,32]{2,1,0:T(8,128)S(1)}, u32[]{:S(2)}, u32[]{:S(2)}) collective-permute-start(f32[1,16,32]{2,1,0:T(8,128)S(1)} %get-tuple-element.192), channel_id=1, source_target_pairs={{0,4},{4,8},{8,12},{12,16},{16,20},{20,24},{24,28},{1,5},{5,9},{9,... | collective-permute-start | bytes 6152 | tf_op jit(solution)/shard_map/ppermute | solution.py:45
  242.3 5.9 %collective-permute-start.35 = (f32[1,16,32]{2,1,0:T(8,128)S(1)}, f32[1,16,32]{2,1,0:T(8,128)S(1)}, u32[]{:S(2)}, u32[]{:S(2)}) collective-permute-start(f32[1,16,32]{2,1,0:T(8,128)S(1)} %get-tuple-element.187), channel_id=1, source_target_pairs={{4,0},{8,4},{12,8},{16,12},{20,16},{24,20},{28,24},{5,1},{9,5},{13... | collective-permute-start | bytes 6152 | tf_op jit(solution)/shard_map/ppermute | solution.py:47
  244.4 6.4 %collective-permute-start.36 = (f32[1,16,32]{2,1,0:T(8,128)S(1)}, f32[1,16,32]{2,1,0:T(8,128)S(1)}, u32[]{:S(2)}, u32[]{:S(2)}) collective-permute-start(f32[1,16,32]{2,1,0:T(8,128)S(1)} %get-tuple-element.186), channel_id=1, source_target_pairs={{0,4},{4,8},{8,12},{12,16},{16,20},{20,24},{24,28},{1,5},{5,9},{9,... | collective-permute-start | bytes 6152 | tf_op jit(solution)/shard_map/ppermute | solution.py:45
  251.1 5.9 %collective-permute-start.37 = (f32[1,16,32]{2,1,0:T(8,128)S(1)}, f32[1,16,32]{2,1,0:T(8,128)S(1)}, u32[]{:S(2)}, u32[]{:S(2)}) collective-permute-start(f32[1,16,32]{2,1,0:T(8,128)S(1)} %get-tuple-element.181), channel_id=1, source_target_pairs={{4,0},{8,4},{12,8},{16,12},{20,16},{24,20},{28,24},{5,1},{9,5},{13... | collective-permute-start | bytes 6152 | tf_op jit(solution)/shard_map/ppermute | solution.py:47
  253.0 6.4 %collective-permute-start.38 = (f32[1,16,32]{2,1,0:T(8,128)S(1)}, f32[1,16,32]{2,1,0:T(8,128)S(1)}, u32[]{:S(2)}, u32[]{:S(2)}) collective-permute-start(f32[1,16,32]{2,1,0:T(8,128)S(1)} %get-tuple-element.180), channel_id=1, source_target_pairs={{0,4},{4,8},{8,12},{12,16},{16,20},{20,24},{24,28},{1,5},{5,9},{9,... | collective-permute-start | bytes 6152 | tf_op jit(solution)/shard_map/ppermute | solution.py:45
  259.6 5.9 %collective-permute-start.39 = (f32[1,16,32]{2,1,0:T(8,128)S(1)}, f32[1,16,32]{2,1,0:T(8,128)S(1)}, u32[]{:S(2)}, u32[]{:S(2)}) collective-permute-start(f32[1,16,32]{2,1,0:T(8,128)S(1)} %get-tuple-element.175), channel_id=1, source_target_pairs={{4,0},{8,4},{12,8},{16,12},{20,16},{24,20},{28,24},{5,1},{9,5},{13... | collective-permute-start | bytes 6152 | tf_op jit(solution)/shard_map/ppermute | solution.py:47
  261.6 6.4 %collective-permute-start.40 = (f32[1,16,32]{2,1,0:T(8,128)S(1)}, f32[1,16,32]{2,1,0:T(8,128)S(1)}, u32[]{:S(2)}, u32[]{:S(2)}) collective-permute-start(f32[1,16,32]{2,1,0:T(8,128)S(1)} %get-tuple-element.174), channel_id=1, source_target_pairs={{0,4},{4,8},{8,12},{12,16},{16,20},{20,24},{24,28},{1,5},{5,9},{9,... | collective-permute-start | bytes 6152 | tf_op jit(solution)/shard_map/ppermute | solution.py:45
  268.2 5.9 %collective-permute-start.41 = (f32[1,16,32]{2,1,0:T(8,128)S(1)}, f32[1,16,32]{2,1,0:T(8,128)S(1)}, u32[]{:S(2)}, u32[]{:S(2)}) collective-permute-start(f32[1,16,32]{2,1,0:T(8,128)S(1)} %get-tuple-element.169), channel_id=1, source_target_pairs={{4,0},{8,4},{12,8},{16,12},{20,16},{24,20},{28,24},{5,1},{9,5},{13... | collective-permute-start | bytes 6152 | tf_op jit(solution)/shard_map/ppermute | solution.py:47
  270.1 6.4 %collective-permute-start.42 = (f32[1,16,32]{2,1,0:T(8,128)S(1)}, f32[1,16,32]{2,1,0:T(8,128)S(1)}, u32[]{:S(2)}, u32[]{:S(2)}) collective-permute-start(f32[1,16,32]{2,1,0:T(8,128)S(1)} %get-tuple-element.168), channel_id=1, source_target_pairs={{0,4},{4,8},{8,12},{12,16},{16,20},{20,24},{24,28},{1,5},{5,9},{9,... | collective-permute-start | bytes 6152 | tf_op jit(solution)/shard_map/ppermute | solution.py:45
  276.8 5.9 %collective-permute-start.43 = (f32[1,16,32]{2,1,0:T(8,128)S(1)}, f32[1,16,32]{2,1,0:T(8,128)S(1)}, u32[]{:S(2)}, u32[]{:S(2)}) collective-permute-start(f32[1,16,32]{2,1,0:T(8,128)S(1)} %get-tuple-element.163), channel_id=1, source_target_pairs={{4,0},{8,4},{12,8},{16,12},{20,16},{24,20},{28,24},{5,1},{9,5},{13... | collective-permute-start | bytes 6152 | tf_op jit(solution)/shard_map/ppermute | solution.py:47
  278.7 6.4 %collective-permute-start.44 = (f32[1,16,32]{2,1,0:T(8,128)S(1)}, f32[1,16,32]{2,1,0:T(8,128)S(1)}, u32[]{:S(2)}, u32[]{:S(2)}) collective-permute-start(f32[1,16,32]{2,1,0:T(8,128)S(1)} %get-tuple-element.162), channel_id=1, source_target_pairs={{0,4},{4,8},{8,12},{12,16},{16,20},{20,24},{24,28},{1,5},{5,9},{9,... | collective-permute-start | bytes 6152 | tf_op jit(solution)/shard_map/ppermute | solution.py:45
  285.5 5.9 %collective-permute-start.45 = (f32[1,16,32]{2,1,0:T(8,128)S(1)}, f32[1,16,32]{2,1,0:T(8,128)S(1)}, u32[]{:S(2)}, u32[]{:S(2)}) collective-permute-start(f32[1,16,32]{2,1,0:T(8,128)S(1)} %get-tuple-element.161), channel_id=1, source_target_pairs={{4,0},{8,4},{12,8},{16,12},{20,16},{24,20},{28,24},{5,1},{9,5},{13... | collective-permute-start | bytes 6152 | tf_op jit(solution)/shard_map/ppermute | solution.py:47
  287.4 6.4 %collective-permute-start.46 = (f32[1,16,32]{2,1,0:T(8,128)S(1)}, f32[1,16,32]{2,1,0:T(8,128)S(1)}, u32[]{:S(2)}, u32[]{:S(2)}) collective-permute-start(f32[1,16,32]{2,1,0:T(8,128)S(1)} %get-tuple-element.160), channel_id=1, source_target_pairs={{0,4},{4,8},{8,12},{12,16},{16,20},{20,24},{24,28},{1,5},{5,9},{9,... | collective-permute-start | bytes 6152 | tf_op jit(solution)/shard_map/ppermute | solution.py:45
  294.3 5.9 %collective-permute-start.48 = (f32[1,1,8,64]{3,2,1,0:T(8,128)S(1)}, f32[1,1,8,64]{3,2,1,0:T(8,128)S(1)}, u32[]{:S(2)}, u32[]{:S(2)}) collective-permute-start(f32[1,1,8,64]{3,2,1,0:T(8,128)S(1)} %get-tuple-element.153), channel_id=1, source_target_pairs={{4,0},{8,4},{12,8},{16,12},{20,16},{24,20},{28,24},{5,1},{9,5},{13... | collective-permute-start | bytes 6152 | tf_op jit(solution)/shard_map/ppermute | solution.py:47
  296.2 6.4 %collective-permute-start.47 = (f32[1,1,8,64]{3,2,1,0:T(8,128)S(1)}, f32[1,1,8,64]{3,2,1,0:T(8,128)S(1)}, u32[]{:S(2)}, u32[]{:S(2)}) collective-permute-start(f32[1,1,8,64]{3,2,1,0:T(8,128)S(1)} %get-tuple-element.152), channel_id=1, source_target_pairs={{0,4},{4,8},{8,12},{12,16},{16,20},{20,24},{24,28},{1,5},{5,9},{9,... | collective-permute-start | bytes 6152 | tf_op jit(solution)/shard_map/ppermute | solution.py:45
  309.9 5.9 %collective-permute-start.52 = (f32[1,1,8,64]{3,2,1,0:T(8,128)S(1)}, f32[1,1,8,64]{3,2,1,0:T(8,128)S(1)}, u32[]{:S(2)}, u32[]{:S(2)}) collective-permute-start(f32[1,1,8,64]{3,2,1,0:T(8,128)S(1)} %get-tuple-element.151), channel_id=1, source_target_pairs={{4,0},{8,4},{12,8},{16,12},{20,16},{24,20},{28,24},{5,1},{9,5},{13... | collective-permute-start | bytes 6152 | tf_op jit(solution)/shard_map/ppermute | solution.py:47
  311.8 6.4 %collective-permute-start.51 = (f32[1,1,8,64]{3,2,1,0:T(8,128)S(1)}, f32[1,1,8,64]{3,2,1,0:T(8,128)S(1)}, u32[]{:S(2)}, u32[]{:S(2)}) collective-permute-start(f32[1,1,8,64]{3,2,1,0:T(8,128)S(1)} %get-tuple-element.150), channel_id=1, source_target_pairs={{0,4},{4,8},{8,12},{12,16},{16,20},{20,24},{24,28},{1,5},{5,9},{9,... | collective-permute-start | bytes 6152 | tf_op jit(solution)/shard_map/ppermute | solution.py:45
  325.4 5.9 %collective-permute-start.56 = (f32[1,1,8,64]{3,2,1,0:T(8,128)S(1)}, f32[1,1,8,64]{3,2,1,0:T(8,128)S(1)}, u32[]{:S(2)}, u32[]{:S(2)}) collective-permute-start(f32[1,1,8,64]{3,2,1,0:T(8,128)S(1)} %get-tuple-element.149), channel_id=1, source_target_pairs={{4,0},{8,4},{12,8},{16,12},{20,16},{24,20},{28,24},{5,1},{9,5},{13... | collective-permute-start | bytes 6152 | tf_op jit(solution)/shard_map/ppermute | solution.py:47
  327.4 6.4 %collective-permute-start.55 = (f32[1,1,8,64]{3,2,1,0:T(8,128)S(1)}, f32[1,1,8,64]{3,2,1,0:T(8,128)S(1)}, u32[]{:S(2)}, u32[]{:S(2)}) collective-permute-start(f32[1,1,8,64]{3,2,1,0:T(8,128)S(1)} %get-tuple-element.148), channel_id=1, source_target_pairs={{0,4},{4,8},{8,12},{12,16},{16,20},{20,24},{24,28},{1,5},{5,9},{9,... | collective-permute-start | bytes 6152 | tf_op jit(solution)/shard_map/ppermute | solution.py:45
  342.0 5.9 %collective-permute-start.60 = (f32[1,1,16,128]{3,2,1,0:T(8,128)S(1)}, f32[1,1,16,128]{3,2,1,0:T(8,128)S(1)}, u32[]{:S(2)}, u32[]{:S(2)}) collective-permute-start(f32[1,1,16,128]{3,2,1,0:T(8,128)S(1)} %get-tuple-element.103), channel_id=1, source_target_pairs={{4,0},{8,4},{12,8},{16,12},{20,16},{24,20},{28,24},{5,1},{9,5},{13... | collective-permute-start | bytes 24584 | tf_op jit(solution)/shard_map/ppermute | solution.py:47
  343.9 6.4 %collective-permute-start.59 = (f32[1,1,16,128]{3,2,1,0:T(8,128)S(1)}, f32[1,1,16,128]{3,2,1,0:T(8,128)S(1)}, u32[]{:S(2)}, u32[]{:S(2)}) collective-permute-start(f32[1,1,16,128]{3,2,1,0:T(8,128)S(1)} %get-tuple-element.102), channel_id=1, source_target_pairs={{0,4},{4,8},{8,12},{12,16},{16,20},{20,24},{24,28},{1,5},{5,9},{9,... | collective-permute-start | bytes 24584 | tf_op jit(solution)/shard_map/ppermute | solution.py:45
  357.8 5.9 %collective-permute-start.64 = (f32[1,1,16,128]{3,2,1,0:T(8,128)S(1)}, f32[1,1,16,128]{3,2,1,0:T(8,128)S(1)}, u32[]{:S(2)}, u32[]{:S(2)}) collective-permute-start(f32[1,1,16,128]{3,2,1,0:T(8,128)S(1)} %get-tuple-element.101), channel_id=1, source_target_pairs={{4,0},{8,4},{12,8},{16,12},{20,16},{24,20},{28,24},{5,1},{9,5},{13... | collective-permute-start | bytes 24584 | tf_op jit(solution)/shard_map/ppermute | solution.py:47
  359.7 6.4 %collective-permute-start.63 = (f32[1,1,16,128]{3,2,1,0:T(8,128)S(1)}, f32[1,1,16,128]{3,2,1,0:T(8,128)S(1)}, u32[]{:S(2)}, u32[]{:S(2)}) collective-permute-start(f32[1,1,16,128]{3,2,1,0:T(8,128)S(1)} %get-tuple-element.100), channel_id=1, source_target_pairs={{0,4},{4,8},{8,12},{12,16},{16,20},{20,24},{24,28},{1,5},{5,9},{9,... | collective-permute-start | bytes 24584 | tf_op jit(solution)/shard_map/ppermute | solution.py:45
  373.6 5.9 %collective-permute-start.68 = (f32[1,1,16,128]{3,2,1,0:T(8,128)S(1)}, f32[1,1,16,128]{3,2,1,0:T(8,128)S(1)}, u32[]{:S(2)}, u32[]{:S(2)}) collective-permute-start(f32[1,1,16,128]{3,2,1,0:T(8,128)S(1)} %get-tuple-element.99), channel_id=1, source_target_pairs={{4,0},{8,4},{12,8},{16,12},{20,16},{24,20},{28,24},{5,1},{9,5},{13... | collective-permute-start | bytes 24584 | tf_op jit(solution)/shard_map/ppermute | solution.py:47
  375.5 6.4 %collective-permute-start.67 = (f32[1,1,16,128]{3,2,1,0:T(8,128)S(1)}, f32[1,1,16,128]{3,2,1,0:T(8,128)S(1)}, u32[]{:S(2)}, u32[]{:S(2)}) collective-permute-start(f32[1,1,16,128]{3,2,1,0:T(8,128)S(1)} %get-tuple-element.98), channel_id=1, source_target_pairs={{0,4},{4,8},{8,12},{12,16},{16,20},{20,24},{24,28},{1,5},{5,9},{9,... | collective-permute-start | bytes 24584 | tf_op jit(solution)/shard_map/ppermute | solution.py:45
  (25 other events, 131.7 us)
